TPU v7x, 512 devices: a whole 4x4x16 slice. The times are simulated.
512 devices in a mesh: req: 8 (over z_lo), row: 8 (over x, core), col: 8 (over y, z_hi).
Axes of the slice: x: 4, y: 4, z: 16 (z_hi: 2, z_lo: 8; z = z_hi * 8 + z_lo), core: 2. Of those that a mesh axis runs over, the one named last changes fastest.
Arguments:
- tokens: bfloat16 [1792, 32768], P('col', ('req', 'row')), may hold values from -6 to 6
- qkv_weight: bfloat16 [1792, 2304], P('col', 'row'), may hold values from -0.125 to 0.125
- out_weight: bfloat16 [1792, 1792], P('row', 'col'), may hold values from -0.125 to 0.125
- head_gain: float32 [1792], P('row'), may hold values from 0.1 to 1.9
- prefix_keys: bfloat16 [24, 256, 8192], P('req', 'row', 'col'), may hold values from -6 to 6
- prefix_values: bfloat16 [24, 1792, 8192], P('req', 'row', 'col'), may hold values from -6 to 6
- suffix_len: int32 [64], P(('req', 'col')), may hold values from 1 to 512, 24576 in all
- prefix_owner: int32 [64], P(('req', 'col')), may hold values from 0 to 23
Outputs:
- layer_out: bfloat16 [1792, 32768], P('col', ('req', 'row'))
Inputs may be any that keep to these rules, and one draw needn't show every extreme that they name: `suffix_len`: the longest suffix has exactly 512 live tokens.
All inputs are finite; a program needn't handle non-finite values. No bound on the sum of `suffix_len` on one device may be relied on, other than what follows from the above.
Results may differ from a plain program's by a relative error of at most 0.015.
Values may be sent and summed in bfloat16 or wider, within the bound.
No kernel may reach another device: no remote copies, remote signals or barrier semaphores. Data moves between devices by JAX's collectives and lax.ppermute only.
A program may use at most 64 MiB of HBM per device.

v0:
```python
import jax
import jax.numpy as jnp
import numpy as np
from jax import lax
from jax.sharding import Mesh, PartitionSpec as P

FEAT = 16
SLOTS = 512
HD = 112
ROW = ("x", "c")
COL = ("y", "zh")
epsilon = 1e-05


def feature_map(values_in):
    feature_count = values_in.shape[-1]
    squares = (values_in[..., :, None] * values_in[..., None, :]).reshape(
        values_in.shape[:-1] + (feature_count * feature_count,)
    )
    constant = jnp.ones(values_in.shape[:-1] + (1,), jnp.float32)
    linear = values_in * feature_count ** (-0.25)
    quadratic = squares * (0.5**0.5 / feature_count**0.5)
    return jnp.concatenate([constant, linear, quadratic], axis=-1).astype(jnp.bfloat16)


def feature_columns(values_in):
    feature_count = values_in.shape[-2]
    length = values_in.shape[-1]
    squares = (values_in[..., :, None, :] * values_in[..., None, :, :]).reshape(
        values_in.shape[:-2] + (feature_count * feature_count, length)
    )
    constant = jnp.ones(values_in.shape[:-2] + (1, length), jnp.float32)
    linear = values_in * feature_count ** (-0.25)
    quadratic = squares * (0.5**0.5 / feature_count**0.5)
    return jnp.concatenate([constant, linear, quadratic], axis=-2).astype(jnp.bfloat16)


def shards(
    tokens, qkv_weight, out_weight, head_gain, prefix_keys, prefix_values, suffix_len, prefix_owner
):
    n_col = lax.psum(1, COL)
    heads_here = head_gain.shape[0] // HD
    partial_proj = lax.dot_general(
        lax.all_gather(tokens, ROW, axis=1, tiled=True),
        qkv_weight,
        (((0,), (0,)), ((), ())),
        preferred_element_type=jnp.float32,
    ).astype(jnp.bfloat16)
    projected = lax.psum_scatter(partial_proj, "y", scatter_dimension=0, tiled=True)
    projected = lax.psum_scatter(projected, "zh", scatter_dimension=0, tiled=True)
    projected = projected.reshape(SLOTS, heads_here, 2 * FEAT + HD)
    queries = projected[..., :FEAT]
    keys_now = projected[..., FEAT : 2 * FEAT]
    values_now = projected[..., 2 * FEAT :]
    pref_here = prefix_keys.shape[0]
    plen_here = prefix_keys.shape[2]
    feats_cached = feature_columns(
        prefix_keys.reshape(pref_here, heads_here, FEAT, plen_here).astype(jnp.float32)
    )
    values_cached = prefix_values.reshape(pref_here, heads_here, HD, plen_here)
    partial_state = jnp.einsum(
        "phet,phvt->phev", feats_cached, values_cached, preferred_element_type=jnp.float32
    )
    state_shape = partial_state.shape[1:]
    piece = partial_state[0].size // n_col
    pieces = partial_state.astype(jnp.bfloat16).reshape(pref_here, n_col, piece)
    pieces = jnp.swapaxes(pieces, 0, 1)
    pieces = lax.psum_scatter(pieces, "y", scatter_dimension=0, tiled=True)
    pieces = lax.psum_scatter(pieces, "zh", scatter_dimension=0, tiled=True)
    pieces = lax.all_gather(pieces[0], "req", axis=0, tiled=True)
    owners = lax.all_gather(prefix_owner, COL, axis=0, tiled=True)
    to_send = jnp.take(pieces, owners, axis=0)
    chosen = lax.all_to_all(to_send, COL, 0, 0, tiled=True)
    chosen = chosen.reshape(state_shape).astype(jnp.float32)
    feats_query = feature_map(queries.astype(jnp.float32)).astype(jnp.float32)
    carried = jnp.einsum("the,hev->thv", feats_query, chosen, precision=lax.Precision.HIGHEST)
    scores = jnp.einsum("thf,shf->hts", queries, keys_now, preferred_element_type=jnp.float32)
    weights = 1.0 + scores * FEAT ** (-0.5) + scores * scores * (0.5 / FEAT)
    positions = jnp.arange(SLOTS, dtype=jnp.int32)
    length = suffix_len[0]
    allowed = (positions[None, :] <= positions[:, None]) & (positions[None, :] < length)
    weights = jnp.where(allowed[None], weights, 0.0).astype(jnp.bfloat16)
    within = jnp.einsum("hts,shv->thv", weights, values_now, preferred_element_type=jnp.float32)
    active = (positions < length)[:, None, None]
    attended = jnp.where(active, carried + within, 0.0)
    inverse_rms = lax.rsqrt(jnp.mean(attended * attended, axis=-1, keepdims=True) + epsilon)
    gains = head_gain.reshape(heads_here, HD)
    normed = (attended * inverse_rms * gains).astype(jnp.bfloat16).reshape(SLOTS, heads_here * HD)
    gathered = lax.all_gather(normed, "zh", axis=0, tiled=True)
    gathered = lax.all_gather(gathered, "y", axis=0, tiled=True)
    out_terms = lax.dot_general(
        out_weight, gathered, (((0,), (1,)), ((), ())), preferred_element_type=jnp.float32
    )
    mixed_sums = lax.psum_scatter(
        out_terms.astype(jnp.bfloat16), ROW, scatter_dimension=1, tiled=True
    ).astype(jnp.float32)
    return (tokens.astype(jnp.float32) + mixed_sums).astype(jnp.bfloat16)


def solution(mesh):
    n_req, n_row, n_col = (mesh.shape[a] for a in ("req", "row", "col"))
    fine = Mesh(
        np.asarray(mesh.devices).reshape(n_req, n_row // 2, 2, n_col // 2, 2),
        ("req", "x", "c", "y", "zh"),
    )
    in_specs = (
        P(COL, ("req",) + ROW),
        P(COL, ROW),
        P(ROW, COL),
        P(ROW),
        P("req", ROW, COL),
        P("req", ROW, COL),
        P(("req",) + COL),
        P(("req",) + COL),
    )
    out_specs = P(COL, ("req",) + ROW)
    return jax.shard_map(shards, mesh=fine, in_specs=in_specs, out_specs=out_specs, check_vma=False)
```

profile of v0, /device:TPU:8, one launch (start us, length us, event | category | flops | bytes accessed | tf_op | source)
XLA Modules:
  0.0 352.4 jit_solution(18403591849002129596)
XLA Ops:
  7.4 1.1 convert.23
  8.4 1.0 multiply_convert_fusion.3
  9.4 0.9 multiply_convert_fusion
  10.3 1.3 fusion.8
  11.7 0.9 reshape.122
  12.6 1.1 copy.14
  14.3 1.3 dynamic-slice.1
  16.2 59.5 %all-reduce.6.cloned.1.call-done = bf16[8,3,7644]{2,1,0:T(4,128)(2,1)} async-done(((bf16[8,3,7644]{2,1,0:T(4,128)(2,1)}), bf16[8,3,7644]{2,1,0:T(4,128)(2,1)}) %all-reduce.6.cloned.1.call-update) | async-done | bytes 366928
  75.8 1.6 constant_dynamic-slice_fusion.1
  77.5 3.7 %convolution_convert_fusion = bf16[4096,288]{0,1:T(8,128)(2,1)} fusion(bf16[224,288]{0,1:T(8,128)(2,1)S(1)} %copy-done.2, bf16[224,4096]{1,0:T(8,128)(2,1)} %all-gather.4.cloned.1.call-done), kind=kOutput, calls=%fused_computation.2 | convolution fusion | flops 529661952 | bytes 4323328 | tf_op jit(solution)/shard_map/dot_general | solution.py:43
  81.9 1.3 dynamic-slice
  83.2 0.7 dynamic-update-slice
  83.9 19.5 %all-reduce = s32[8]{0:T(128)S(1)} all-reduce(s32[8]{0:T(128)S(1)} %dynamic-update-slice), channel_id=1, replica_groups=mesh['req'=8,'x'=4,'c'=2,'y'=4,'zh'=2] {'y','zh'}, use_global_device_ids=true, to_apply=%add | all-reduce | flops 8 | bytes 64
  103.4 1.3 dynamic-slice.3
  104.7 34.3 %all-reduce.8.cloned.1.call-done = bf16[2,3,7644]{2,1,0:T(4,128)(2,1)} async-done(((bf16[2,3,7644]{2,1,0:T(4,128)(2,1)}), bf16[2,3,7644]{2,1,0:T(4,128)(2,1)}) %all-reduce.8.cloned.1.call-update) | async-done | bytes 91744
  139.0 1.5 constant_dynamic-slice_fusion
  140.6 48.8 %all-gather = bf16[1,24,7644]{2,0,1:T(2,128)(2,1)S(1)} all-gather(bf16[1,3,7644]{2,0,1:T(2,128)(2,1)S(1)} %copy.15), channel_id=2, replica_groups=mesh['req'=8,'x'=4,'c'=2,'y'=4,'zh'=2] {'req'}, dimensions={1}, use_global_device_ids=true | all-gather | bytes 412776 | tf_op jit(solution)/shard_map/all_gather | solution.py:70
  189.5 0.6 gather_fusion
  190.8 0.7 reduce.1
  191.4 0.8 reshape.147
  192.3 4.8 %all-to-all-start = ((bf16[8,2,3822]{2,1,0:T(2,128)(2,1)}), bf16[8,2,3822]{2,1,0:T(2,128)(2,1)S(1)}, u32[]{:S(2)}, u32[]{:S(2)}) async-start(bf16[8,2,3822]{2,1,0:T(2,128)(2,1)} %reshape.147), calls=%async_computation | async-start | bytes 245760 | tf_op jit(solution)/shard_map/all_to_all | solution.py:73
  197.9 13.7 %all-to-all-done = bf16[8,2,3822]{2,1,0:T(2,128)(2,1)S(1)} async-done(((bf16[8,2,3822]{2,1,0:T(2,128)(2,1)}), bf16[8,2,3822]{2,1,0:T(2,128)(2,1)S(1)}, u32[]{:S(2)}, u32[]{:S(2)}) %all-to-all-start) | async-done | bytes 122336 | tf_op jit(solution)/shard_map/all_to_all | solution.py:73
  211.8 0.7 reduce
  212.8 23.3 %reduce-scatter.6.cloned.1.call-done = bf16[512,288]{0,1:T(8,128)(2,1)} async-done(((bf16[1024,288]{0,1:T(8,128)(2,1)}), bf16[512,288]{0,1:T(8,128)(2,1)}) %reduce-scatter.6.cloned.1.call-update) | async-done | bytes 294928 | tf_op jit(solution)/shard_map/reduce_scatter | solution.py:50
  236.1 0.8 slice_convert_fusion
  236.8 0.8 multiply_convert_fusion.4
  237.6 1.9 fusion.7
  240.2 28.6 %all_gather.18 = bf16[1024,224]{0,1:T(8,128)(2,1)} all-gather(bf16[512,224]{0,1:T(8,128)(2,1)S(1)} %bitcast.34), channel_id=1, replica_groups=mesh['req'=8,'x'=4,'c'=2,'y'=4,'zh'=2] {'zh'}, dimensions={0}, use_global_device_ids=true | all-gather | bytes 688128 | tf_op jit(solution)/shard_map/all_gather | solution.py:89
  269.0 29.1 %all-gather.6.cloned.1.call-done = bf16[4096,224]{0,1:T(8,128)(2,1)} async-done(((bf16[1024,224]{0,1:T(8,128)(2,1)}), bf16[4096,224]{0,1:T(8,128)(2,1)}) %all-gather.6.cloned.1.call-update) | async-done | bytes 1835024 | tf_op jit(solution)/shard_map/all_gather | solution.py:90
  298.1 3.4 fusion
  301.5 42.1 %reduce-scatter.8.cloned.1.call-done = bf16[224,512]{1,0:T(8,128)(2,1)} async-done(((bf16[224,4096]{1,0:T(8,128)(2,1)}), bf16[224,512]{1,0:T(8,128)(2,1)}) %reduce-scatter.8.cloned.1.call-update) | async-done | bytes 229392 | tf_op jit(solution)/shard_map/reduce_scatter | solution.py:94
  343.6 1.7 add_convert_fusion
  (44 shorter events, 3.0 us)
Async XLA Ops:
  7.4 3.0 copy-start
  7.4 68.4 %all-reduce.6.cloned.1.call-start = ((), (), s32[]{:S(2)}) async-start(), calls=%async_computation.9 | async-start | bytes 983040
  11.6 65.8 %copy-start.2 = (bf16[224,288]{0,1:T(8,128)(2,1)S(1)}, bf16[224,288]{0,1:T(8,128)(2,1)}, u32[]{:S(2)}) copy-start(bf16[224,288]{0,1:T(8,128)(2,1)} %param.9) | copy-start | bytes 387076
  13.7 63.8 %all-gather.4.cloned.1.call-start = ((), (), s32[]{:S(2)}) async-start(), calls=%async_computation.4 | async-start | bytes 2064384 | tf_op jit(solution)/shard_map/all_gather | solution.py:44
  14.2 124.8 %all-reduce.8.cloned.1.call-start = ((), (), s32[]{:S(2)}) async-start(), calls=%async_computation.10 | async-start | bytes 245760
  77.4 112.7 %reduce-scatter.4.cloned.1.call-start = ((), (), s32[]{:S(2)}) async-start(), calls=%async_computation.5 | async-start | bytes 2949120 | tf_op jit(solution)/shard_map/reduce_scatter | solution.py:49
  81.2 154.9 %reduce-scatter.6.cloned.1.call-start = ((), (), s32[]{:S(2)}) async-start(), calls=%async_computation.6 | async-start | bytes 884736 | tf_op jit(solution)/shard_map/reduce_scatter | solution.py:50
  189.4 8.3 %copy-start.4 = (f32[224]{0:T(256)S(1)}, f32[224]{0:T(256)}, u32[]{:S(2)}) copy-start(f32[224]{0:T(256)} %param.11) | copy-start | bytes 2692
  192.3 19.3 %all-to-all-start = ((bf16[8,2,3822]{2,1,0:T(2,128)(2,1)}), bf16[8,2,3822]{2,1,0:T(2,128)(2,1)S(1)}, u32[]{:S(2)}, u32[]{:S(2)}) async-start(bf16[8,2,3822]{2,1,0:T(2,128)(2,1)} %reshape.147), calls=%async_computation | async-start | bytes 245760 | tf_op jit(solution)/shard_map/all_to_all | solution.py:73
  197.1 101.0 %all-gather.6.cloned.1.call-start = ((), (), s32[]{:S(2)}) async-start(), calls=%async_computation.7 | async-start | bytes 2293760 | tf_op jit(solution)/shard_map/all_gather | solution.py:90
  239.5 58.6 %copy-start.3 = (bf16[224,224]{1,0:T(8,128)(2,1)S(1)}, bf16[224,224]{1,0:T(8,128)(2,1)}, u32[]{:S(2)}) copy-start(bf16[224,224]{1,0:T(8,128)(2,1)} %param.10) | copy-start | bytes 301060
  268.9 74.7 %copy-start.1 = (bf16[224,512]{1,0:T(8,128)(2,1)S(1)}, bf16[224,512]{1,0:T(8,128)(2,1)}, u32[]{:S(2)}) copy-start(bf16[224,512]{1,0:T(8,128)(2,1)} %param.8) | copy-start | bytes 688132
  268.9 74.7 %reduce-scatter.8.cloned.1.call-start = ((), (), s32[]{:S(2)}) async-start(), calls=%async_computation.8 | async-start | bytes 2064384 | tf_op jit(solution)/shard_map/reduce_scatter | solution.py:94
Sparse Core Ops, SparseCore 0:
  13.8 61.9 all-reduce.5
  78.6 60.3 all-reduce.7
  141.9 29.7 reduce-scatter.3
  190.3 45.7 reduce-scatter.5
  269.0 28.9 all-gather.5
Sparse Core Ops, SparseCore 1:
  16.3 36.7 all-gather.3
  301.6 42.0 reduce-scatter.7
where the time goes:
time: 353 us; the launch traced here: 352 us
  waiting for transfers between devices  203 us (58%)
  blocking collectives  97 us (27%)
  between operations  16.7 us (5%)
  local copies, waits for them, and re-layouts  12.2 us (3%)
  matrix products  10.8 us (3%)
  other arithmetic  7.93 us (2%)
  starting transfers between devices  5.03 us (1%)
    unnamed x9, waiting for transfers between devices  94.5 us
    all_gather x1, blocking collectives, shards(): pieces = lax.all_gather(pieces[0], 'req', axis=0, tiled=True)  48.8 us
    reduce_scatter x1, waiting for transfers between devices, shards(): lax.psum_scatter(out_terms.astype(jnp.bfloat16), ROW, scatter_dimension=1...  42.1 us
    all_gather x1, waiting for transfers between devices, shards(): gathered = lax.all_gather(gathered, 'y', axis=0, tiled=True)  29.1 us
    all_gather x1, blocking collectives, shards(): gathered = lax.all_gather(normed, 'zh', axis=0, tiled=True)  28.6 us
    reduce_scatter x1, waiting for transfers between devices, shards(): lax.psum_scatter(projected, 'zh', scatter_dimension=0, tiled=True)  23.3 us
    unnamed x1, blocking collectives  19.5 us
    all_to_all x1, waiting for transfers between devices, shards(): chosen = lax.all_to_all(to_send, COL, 0, 0, tiled=True)  13.7 us
  transfers between devices with their start and end apart: 8, of which 6 were waited for; matrix products, arithmetic and copies ran while one was open for 4% of the time, Pallas kernels for 0%

commit v1 on v0

--- a/solution.py
+++ b/solution.py
@@ -10,6 +10,12 @@
 ROW = ("x", "c")
 COL = ("y", "zh")
 epsilon = 1e-05
+make_the_space = lambda z_in, d_out: jnp.concatenate(
+    lax.all_to_all(
+        jnp.stack(lax.psum(1, axis_name="y") * [z_in]), split_axis=0, concat_axis=0, axis_name="y"
+    ),
+    d_out,
+)
 
 
 def feature_map(values_in):
@@ -87,7 +93,7 @@
     gains = head_gain.reshape(heads_here, HD)
     normed = (attended * inverse_rms * gains).astype(jnp.bfloat16).reshape(SLOTS, heads_here * HD)
     gathered = lax.all_gather(normed, "zh", axis=0, tiled=True)
-    gathered = lax.all_gather(gathered, "y", axis=0, tiled=True)
+    gathered = make_the_space(gathered, 0)
     out_terms = lax.dot_general(
         out_weight, gathered, (((0,), (1,)), ((), ())), preferred_element_type=jnp.float32
     )

time: 353 us -> 341 us (0.966)
  the two profiles are of different devices: /device:TPU:8 before, /device:TPU:16 now
where the time goes in v1:
time: 341 us
  waiting for transfers between devices  168 us (49%)
  blocking collectives  120 us (35%)
  between operations  16.7 us (5%)
  local copies, waits for them, and re-layouts  13.2 us (4%)
  matrix products  9.36 us (3%)
  other arithmetic  7.93 us (2%)
  starting transfers between devices  4.98 us (1%)
    unnamed x8, waiting for transfers between devices  96 us
    all_gather x1, blocking collectives, shards(): pieces = lax.all_gather(pieces[0], 'req', axis=0, tiled=True)  48.9 us
    reduce_scatter x1, waiting for transfers between devices, shards(): lax.psum_scatter(out_terms.astype(jnp.bfloat16), ROW, scatter_dimension=1...  35.1 us
    all_gather x1, blocking collectives, shards(): gathered = lax.all_gather(normed, 'zh', axis=0, tiled=True)  28.5 us
    all_to_all x1, blocking collectives, lax.all_to_all(jnp.stack(lax.psum(1, axis_name='y') * [z_in]), split_axis...  25 us
    reduce_scatter x1, waiting for transfers between devices, shards(): lax.psum_scatter(projected, 'zh', scatter_dimension=0, tiled=True)  23.6 us
    unnamed x1, blocking collectives  18 us
    all_to_all x1, waiting for transfers between devices, shards(): chosen = lax.all_to_all(to_send, COL, 0, 0, tiled=True)  13.4 us
  transfers between devices with their start and end apart: 7, of which 5 were waited for; matrix products, arithmetic and copies ran while one was open for 5% of the time, Pallas kernels for 0%

profile of v1, /device:TPU:16, one launch (start us, length us, event | category | flops | bytes accessed | tf_op | source)
XLA Modules:
  0.0 340.7 jit_solution(17626835292777369966)
XLA Ops:
  7.4 1.1 convert.23
  8.4 1.0 multiply_convert_fusion.3
  9.4 0.9 multiply_convert_fusion
  10.3 1.3 fusion.8
  11.7 0.9 reshape.127
  12.6 1.0 copy.16
  14.3 1.3 dynamic-slice.1
  16.2 59.7 %all-reduce.6.cloned.1.call-done = bf16[8,3,7644]{2,1,0:T(4,128)(2,1)} async-done(((bf16[8,3,7644]{2,1,0:T(4,128)(2,1)}), bf16[8,3,7644]{2,1,0:T(4,128)(2,1)}) %all-reduce.6.cloned.1.call-update) | async-done | bytes 366928
  75.9 1.6 constant_dynamic-slice_fusion.1
  77.6 3.7 %convolution_convert_fusion = bf16[4096,288]{0,1:T(8,128)(2,1)} fusion(bf16[224,288]{0,1:T(8,128)(2,1)S(1)} %copy-done.2, bf16[224,4096]{1,0:T(8,128)(2,1)} %all-gather.3.cloned.1.call-done), kind=kOutput, calls=%fused_computation.2 | convolution fusion | flops 529661952 | bytes 4323328 | tf_op jit(solution)/shard_map/dot_general | solution.py:49
  82.0 1.3 dynamic-slice
  83.2 0.7 dynamic-update-slice
  83.9 18.0 %all-reduce = s32[8]{0:T(128)S(1)} all-reduce(s32[8]{0:T(128)S(1)} %dynamic-update-slice), channel_id=1, replica_groups=mesh['req'=8,'x'=4,'c'=2,'y'=4,'zh'=2] {'y','zh'}, use_global_device_ids=true, to_apply=%add | all-reduce | flops 8 | bytes 64
  101.9 1.3 dynamic-slice.3
  103.2 35.7 %all-reduce.8.cloned.1.call-done = bf16[2,3,7644]{2,1,0:T(4,128)(2,1)} async-done(((bf16[2,3,7644]{2,1,0:T(4,128)(2,1)}), bf16[2,3,7644]{2,1,0:T(4,128)(2,1)}) %all-reduce.8.cloned.1.call-update) | async-done | bytes 91744
  138.9 1.4 constant_dynamic-slice_fusion
  140.4 48.9 %all-gather = bf16[1,24,7644]{2,0,1:T(2,128)(2,1)S(1)} all-gather(bf16[1,3,7644]{2,0,1:T(2,128)(2,1)S(1)} %copy.17), channel_id=2, replica_groups=mesh['req'=8,'x'=4,'c'=2,'y'=4,'zh'=2] {'req'}, dimensions={1}, use_global_device_ids=true | all-gather | bytes 412776 | tf_op jit(solution)/shard_map/all_gather | solution.py:76
  190.6 0.7 reduce.1
  191.3 0.8 reshape.153
  192.1 4.8 %all-to-all-start = ((bf16[8,2,3822]{2,1,0:T(2,128)(2,1)}), bf16[8,2,3822]{2,1,0:T(2,128)(2,1)S(1)}, u32[]{:S(2)}, u32[]{:S(2)}) async-start(bf16[8,2,3822]{2,1,0:T(2,128)(2,1)} %reshape.153), calls=%async_computation | async-start | bytes 245760 | tf_op jit(solution)/shard_map/all_to_all | solution.py:79
  197.7 13.4 %all-to-all-done = bf16[8,2,3822]{2,1,0:T(2,128)(2,1)S(1)} async-done(((bf16[8,2,3822]{2,1,0:T(2,128)(2,1)}), bf16[8,2,3822]{2,1,0:T(2,128)(2,1)S(1)}, u32[]{:S(2)}, u32[]{:S(2)}) %all-to-all-start) | async-done | bytes 122336 | tf_op jit(solution)/shard_map/all_to_all | solution.py:79
  211.3 0.7 reduce
  212.3 23.6 %reduce-scatter.6.cloned.1.call-done = bf16[512,288]{0,1:T(8,128)(2,1)} async-done(((bf16[1024,288]{0,1:T(8,128)(2,1)}), bf16[512,288]{0,1:T(8,128)(2,1)}) %reduce-scatter.6.cloned.1.call-update) | async-done | bytes 294928 | tf_op jit(solution)/shard_map/reduce_scatter | solution.py:56
  235.9 0.8 slice_convert_fusion
  236.7 0.8 multiply_convert_fusion.4
  237.4 1.9 fusion.7
  240.1 28.5 %all_gather.15 = bf16[1024,224]{0,1:T(8,128)(2,1)S(1)} all-gather(bf16[512,224]{0,1:T(8,128)(2,1)S(1)} %bitcast.38), channel_id=1, replica_groups=mesh['req'=8,'x'=4,'c'=2,'y'=4,'zh'=2] {'zh'}, dimensions={0}, use_global_device_ids=true | all-gather | bytes 688128 | tf_op jit(solution)/shard_map/all_gather | solution.py:95
  268.8 25.0 %all_to_all.11 = bf16[4,1024,224]{1,2,0:T(8,128)(2,1)S(1)} all-to-all(bf16[4,1024,224]{1,2,0:T(8,128)(2,1)S(1)} %stack.2), channel_id=1, replica_groups=mesh['req'=8,'x'=4,'c'=2,'y'=4,'zh'=2] {'y'}, dimensions={0} | all-to-all | bytes 3670016 | tf_op jit(solution)/shard_map/all_to_all | solution.py:14
  294.0 0.7 copy-done.3
  294.7 2.0 fusion
  296.7 35.1 %reduce-scatter.8.cloned.1.call-done = bf16[224,512]{1,0:T(8,128)(2,1)} async-done(((bf16[224,4096]{1,0:T(8,128)(2,1)}), bf16[224,512]{1,0:T(8,128)(2,1)}) %reduce-scatter.8.cloned.1.call-update) | async-done | bytes 229392 | tf_op jit(solution)/shard_map/reduce_scatter | solution.py:100
  331.9 1.7 add_convert_fusion
  (44 shorter events, 4.0 us)
Async XLA Ops:
  7.4 3.0 copy-start
  7.4 68.5 %all-reduce.6.cloned.1.call-start = ((), (), s32[]{:S(2)}) async-start(), calls=%async_computation.9 | async-start | bytes 983040
  11.6 65.9 %copy-start.2 = (bf16[224,288]{0,1:T(8,128)(2,1)S(1)}, bf16[224,288]{0,1:T(8,128)(2,1)}, u32[]{:S(2)}) copy-start(bf16[224,288]{0,1:T(8,128)(2,1)} %param.9) | copy-start | bytes 387076
  13.6 63.9 %all-gather.3.cloned.1.call-start = ((), (), s32[]{:S(2)}) async-start(), calls=%async_computation.5 | async-start | bytes 2064384 | tf_op jit(solution)/shard_map/all_gather | solution.py:50
  14.2 124.7 %all-reduce.8.cloned.1.call-start = ((), (), s32[]{:S(2)}) async-start(), calls=%async_computation.10 | async-start | bytes 245760
  77.5 112.5 %reduce-scatter.4.cloned.1.call-start = ((), (), s32[]{:S(2)}) async-start(), calls=%async_computation.6 | async-start | bytes 2949120 | tf_op jit(solution)/shard_map/reduce_scatter | solution.py:55
  81.3 154.6 %reduce-scatter.6.cloned.1.call-start = ((), (), s32[]{:S(2)}) async-start(), calls=%async_computation.7 | async-start | bytes 884736 | tf_op jit(solution)/shard_map/reduce_scatter | solution.py:56
  189.3 8.3 %copy-start.4 = (f32[224]{0:T(256)S(1)}, f32[224]{0:T(256)}, u32[]{:S(2)}) copy-start(f32[224]{0:T(256)} %param.11) | copy-start | bytes 2692
  192.1 19.0 %all-to-all-start = ((bf16[8,2,3822]{2,1,0:T(2,128)(2,1)}), bf16[8,2,3822]{2,1,0:T(2,128)(2,1)S(1)}, u32[]{:S(2)}, u32[]{:S(2)}) async-start(bf16[8,2,3822]{2,1,0:T(2,128)(2,1)} %reshape.153), calls=%async_computation | async-start | bytes 245760 | tf_op jit(solution)/shard_map/all_to_all | solution.py:79
  196.9 134.9 %reduce-scatter.8.cloned.1.call-start = ((), (), s32[]{:S(2)}) async-start(), calls=%async_computation.8 | async-start | bytes 2064384 | tf_op jit(solution)/shard_map/reduce_scatter | solution.py:100
  293.8 0.9 copy-start.3
  294.7 37.1 %copy-start.1 = (bf16[224,512]{1,0:T(8,128)(2,1)S(1)}, bf16[224,512]{1,0:T(8,128)(2,1)}, u32[]{:S(2)}) copy-start(bf16[224,512]{1,0:T(8,128)(2,1)} %param.8) | copy-start | bytes 688132
Sparse Core Ops, SparseCore 0:
  13.8 62.0 all-reduce.5
  78.7 60.1 all-reduce.7
  141.8 29.4 reduce-scatter.3
  190.1 45.7 reduce-scatter.5
Sparse Core Ops, SparseCore 1:
  16.3 36.6 all-gather.2
  296.8 35.0 reduce-scatter.7
